TPU v7x, 256 devices: a whole 4x4x8 slice. The times are simulated.
256 devices in a mesh: lat: 8 (over y, z_lo), lon: 8 (over x, core), dp: 4 (over z_hi).
Axes of the slice: x: 4, y: 4, z: 8 (z_hi: 4, z_lo: 2; z = z_hi * 2 + z_lo), core: 2. Of those that a mesh axis runs over, the one named last changes fastest.
Arguments:
- state_grid: bfloat16 [4, 384, 768, 128], P('dp', ('lat', 'lon')), may hold values from -6 to 6
- cotangent: bfloat16 [4, 384, 768, 128], P('dp', ('lat', 'lon')), may hold values from -6 to 6
- legendre: bfloat16 [384, 384, 384], P(('lat', 'lon')), may hold values from -0.3125 to 0.3125
- wave_ids: int32 [384], replicated, may hold values from 0 to 383, each once
- weights: bfloat16 [384, 2, 4, 1024], P('lat'), may hold values from -0.75 to 0.75
Outputs:
- input_grad: bfloat16 [4, 384, 768, 128], P('dp', ('lat', 'lon'))
- weight_grad: float32 [384, 2, 4, 1024], P('lat')
Inputs may be any that keep to these rules, and one draw needn't show every extreme that they name: wave_ids[j] is the wavenumber of slot j; each of 0 to 383 stands in exactly one slot.
All inputs are finite; a program needn't handle non-finite values.
Results may differ from a plain program's by a relative error of at most 0.034.
Values may be sent and summed in bfloat16 or wider, within the bound.
No kernel may reach another device: no remote copies, remote signals or barrier semaphores. Data moves between devices by JAX's collectives and lax.ppermute only.
A program may use at most 128 MiB of HBM per device.

v0:
```python
import math

import jax
import jax.numpy as jnp
from jax import lax
from jax.sharding import PartitionSpec as P

NLON = 768
GROUPS = 4
GROUP_WIDTH = 32


def build_tables(wave_ids):
    slots = wave_ids.shape[0]
    columns = jnp.arange(NLON, dtype=jnp.int32)
    phase_int = wave_ids[:, None] * columns[None, :] % NLON
    angles = phase_int.astype(jnp.float32) * jnp.float32(2.0 * math.pi / NLON)
    factor = jnp.float32(1.0 / math.sqrt(NLON))
    parts = jnp.concatenate(
        [(jnp.cos(angles) * factor).astype(jnp.bfloat16), (-jnp.sin(angles) * factor).astype(jnp.bfloat16)],
        axis=0,
    )
    table_row = lax.broadcasted_iota(jnp.int32, (2 * slots, 2 * slots), 0)
    part_row = lax.broadcasted_iota(jnp.int32, (2 * slots, 2 * slots), 1)
    interleave = (table_row == 2 * (part_row % slots) + part_row // slots).astype(jnp.bfloat16)
    forward_table = jnp.einsum(
        "kj,jn->kn", interleave, parts, preferred_element_type=jnp.float32
    ).astype(jnp.bfloat16)
    doubling = jnp.where(wave_ids == 0, 1.0, 2.0).astype(jnp.bfloat16)
    inverse_table = forward_table * jnp.repeat(doubling, 2)[:, None]
    return (forward_table, inverse_table)


def block_diagonal(weights):
    degree_count = weights.shape[0]
    width = GROUPS * GROUP_WIDTH
    parts = weights.reshape(degree_count, 2, width, GROUP_WIDTH)
    spread = jnp.tile(parts, (1, 1, 1, GROUPS))
    rows = lax.broadcasted_iota(jnp.int32, (width, width), 0) // GROUP_WIDTH
    cols = lax.broadcasted_iota(jnp.int32, (width, width), 1) // GROUP_WIDTH
    blocks = jnp.where(rows == cols, spread, jnp.zeros((), weights.dtype))
    return blocks[:, 0], blocks[:, 1]


def build_kernel(weights):
    degree_count = weights.shape[0]
    real_part = weights[:, 0].reshape(degree_count, GROUPS, GROUP_WIDTH, GROUP_WIDTH)
    imag_part = weights[:, 1].reshape(degree_count, GROUPS, GROUP_WIDTH, GROUP_WIDTH)
    upper_rows = jnp.stack([real_part, imag_part], axis=3)
    lower_rows = jnp.stack([-imag_part, real_part], axis=3)
    return jnp.stack([upper_rows, lower_rows], axis=2)


def gelu_slope(branch):
    normal_cdf = 0.5 * (1.0 + lax.erf(branch * (1.0 / math.sqrt(2.0))))
    density = jnp.exp(-0.5 * branch * branch) * (1.0 / math.sqrt(2.0 * math.pi))
    return normal_cdf + branch * density


def gather_sum(values, sum_axis, gather_axes):
    parts = lax.axis_size(sum_axis)
    count = 1
    for name in gather_axes:
        count *= lax.axis_size(name)
    rows = values.reshape(-1, values.shape[-1])
    chunks = rows.reshape(parts, rows.shape[0] // parts, rows.shape[1])
    scattered = lax.all_to_all(chunks, sum_axis, split_axis=0, concat_axis=0, tiled=True)
    reduced = jnp.sum(scattered.astype(jnp.float32), axis=0).astype(values.dtype)
    tiled = jnp.broadcast_to(reduced[None], (count,) + reduced.shape)
    gathered = lax.all_to_all(tiled, gather_axes, split_axis=0, concat_axis=0, tiled=True)
    return gathered.reshape(-1, values.shape[-1])


def reduce_over(values, axes):
    count = 1
    for name in axes:
        count *= lax.axis_size(name)
    rows = values.reshape(-1, values.shape[-1])
    chunks = rows.reshape(count, rows.shape[0] // count, rows.shape[1])
    scattered = lax.all_to_all(chunks, axes, split_axis=0, concat_axis=0, tiled=True)
    reduced = jnp.sum(scattered.astype(jnp.float32), axis=0).astype(values.dtype)
    tiled = jnp.broadcast_to(reduced[None], (count,) + reduced.shape)
    gathered = lax.all_to_all(tiled, axes, split_axis=0, concat_axis=0, tiled=True)
    return gathered.reshape(values.shape)


def shards(state_grid, cotangent, legendre, wave_ids, weights):
    lat_count = lax.axis_size("lat")
    lon_count = lax.axis_size("lon")
    samples, rows_dev, lon_cells, channels = state_grid.shape
    slot_count, lat_cells, degree_count = legendre.shape
    slot_reals = 2 * slot_count
    first_slot = (lax.axis_index("lat") * lon_count + lax.axis_index("lon")) * slot_count
    held_waves = lax.dynamic_slice_in_dim(wave_ids, first_slot, slot_count)
    degree_ids = jnp.arange(degree_count, dtype=jnp.int32)
    masked = jnp.where(
        degree_ids[None, None, :] >= held_waves[:, None, None],
        legendre,
        jnp.zeros((), legendre.dtype),
    )
    forward_table, inverse_table = build_tables(wave_ids)

    def analyze(source, twiddle):
        spectra = jnp.einsum(
            "srnc,kn->srkc", source, twiddle, preferred_element_type=jnp.float32
        ).astype(jnp.bfloat16)
        gathered = lax.all_to_all(spectra, ("lat", "lon"), split_axis=2, concat_axis=1, tiled=True)
        blocks = gathered.reshape(samples, lat_cells, slot_count, 2 * channels)
        spectral = jnp.einsum("samc,mal->slmc", blocks, masked, preferred_element_type=jnp.float32)
        peers = lat_count * lon_count
        spectral = spectral.astype(jnp.bfloat16).reshape(
            peers, degree_count // peers, slot_count, 2 * channels
        )
        return lax.all_to_all(spectral, ("lat", "lon"), split_axis=0, concat_axis=0, tiled=True)

    def synthesize(spectral, twiddle):
        joined = lax.all_to_all(spectral, ("lat", "lon"), split_axis=0, concat_axis=0, tiled=True)
        blocks = joined.reshape(samples, degree_count, slot_count, 2 * channels)
        spectra = jnp.einsum(
            "slmc,mal->samc", blocks, masked, preferred_element_type=jnp.float32
        ).astype(jnp.bfloat16)
        spectra = spectra.reshape(samples, lat_cells, slot_reals, channels)
        pencil = lax.all_to_all(spectra, ("lat", "lon"), split_axis=1, concat_axis=2, tiled=True)
        return jnp.einsum("srkc,kn->srnc", pencil, twiddle, preferred_element_type=jnp.float32)

    coef_rows = analyze(state_grid, forward_table)
    held_count = weights.shape[0] // lon_count
    held_weights = lax.dynamic_slice_in_dim(weights, lax.axis_index("lon") * held_count, held_count)
    real_bd, imag_bd = block_diagonal(held_weights)
    mixing = jnp.concatenate(
        [
            jnp.concatenate([real_bd, imag_bd], axis=2),
            jnp.concatenate([-imag_bd, real_bd], axis=2),
        ],
        axis=1,
    )
    mixed_rows = jnp.einsum(
        "slmc,lcd->slmd", coef_rows, mixing, preferred_element_type=jnp.float32
    ).astype(jnp.bfloat16)
    branch = synthesize(mixed_rows, inverse_table)
    pulled = (cotangent.astype(jnp.float32) * gelu_slope(branch)).astype(jnp.bfloat16)
    back_rows = analyze(pulled, inverse_table)
    pair_products = jnp.einsum(
        "slmc,slmd->lcd", coef_rows, back_rows, preferred_element_type=jnp.float32
    )
    width = GROUPS * GROUP_WIDTH
    same_part = pair_products[:, :width, :width] + pair_products[:, width:, width:]
    cross_part = pair_products[:, :width, width:] - pair_products[:, width:, :width]
    grad_full = jnp.concatenate([same_part, cross_part], axis=2)
    rows_group = lax.broadcasted_iota(jnp.int32, (width, 2 * width), 0) // GROUP_WIDTH
    cols_group = lax.broadcasted_iota(jnp.int32, (width, 2 * width), 1) % width // GROUP_WIDTH
    grad_terms = jnp.where(
        rows_group == cols_group, grad_full.astype(jnp.bfloat16), jnp.zeros((), jnp.bfloat16)
    )
    pick_in = lax.broadcasted_iota(jnp.int32, (2 * width, 2 * GROUP_WIDTH), 0)
    pick_out = lax.broadcasted_iota(jnp.int32, (2 * width, 2 * GROUP_WIDTH), 1)
    picker = (
        (pick_in // width == pick_out // GROUP_WIDTH)
        & (pick_in % GROUP_WIDTH == pick_out % GROUP_WIDTH)
    ).astype(jnp.bfloat16)
    compact = jnp.einsum("lcd,de->lce", grad_terms, picker, preferred_element_type=jnp.float32)
    local_grad = (
        compact.reshape(held_count, GROUPS, GROUP_WIDTH, 2, GROUP_WIDTH)
        .transpose(0, 3, 1, 2, 4)
        .reshape(held_weights.shape)
    )
    weight_grad = gather_sum(local_grad.astype(jnp.bfloat16), "dp", ("lon", "dp"))
    weight_grad = weight_grad.reshape(weights.shape).astype(jnp.float32)
    demixed_rows = jnp.einsum(
        "slmd,lcd->slmc", back_rows, mixing, preferred_element_type=jnp.float32
    ).astype(jnp.bfloat16)
    returned = synthesize(demixed_rows, forward_table)
    input_grad = (cotangent.astype(jnp.float32) + returned).astype(jnp.bfloat16)
    return (input_grad, weight_grad)


def solution(mesh):
    return jax.shard_map(
        shards,
        mesh=mesh,
        in_specs=(
            P("dp", ("lat", "lon"), None, None),
            P("dp", ("lat", "lon"), None, None),
            P(("lat", "lon"), None, None),
            P(),
            P("lat", None, None, None),
        ),
        out_specs=(P("dp", ("lat", "lon"), None, None), P("lat", None, None, None)),
        check_vma=False,
    )
```

profile of v0, /device:TPU:1, one launch (start us, length us, event | category | flops | bytes accessed | tf_op | source)
XLA Modules:
  0.0 327.4 jit_solution(17771193169506495913)
XLA Ops:
  0.7 6.3 %multiply_convert_fusion.1 = (bf16[384,768]{1,0:T(8,128)(2,1)S(1)}, bf16[384,768]{1,0:T(8,128)(2,1)S(1)}) fusion(s32[384]{0:T(512)} %param.8), kind=kLoop, calls=%fused_computation.53 | loop fusion | flops 4128768 | bytes 1181184 | tf_op jit(solution)/shard_map/convert_element_type | solution.py:20
  6.9 1.2 fusion.10
  8.2 1.1 fusion.13
  9.3 2.0 copy.40
  11.2 10.5 %all-to-all-start = ((bf16[1,6,768,128]{3,1,0,2:T(8,128)(2,1)}), bf16[1,6,768,128]{3,1,0,2:T(8,128)(2,1)S(1)}, u32[]{:S(2)}, u32[]{:S(2)}) async-start(bf16[1,6,768,128]{3,1,0,2:T(8,128)(2,1)} %copy.40), calls=%async_computation | async-start | bytes 3145728 | tf_op jit(solution)/shard_map/all_to_all | solution.py:107
  21.9 23.3 %all-to-all-done = bf16[1,6,768,128]{3,1,0,2:T(8,128)(2,1)S(1)} async-done(((bf16[1,6,768,128]{3,1,0,2:T(8,128)(2,1)}), bf16[1,6,768,128]{3,1,0,2:T(8,128)(2,1)S(1)}, u32[]{:S(2)}, u32[]{:S(2)}) %all-to-all-start) | async-done | bytes 1179680 | tf_op jit(solution)/shard_map/all_to_all | solution.py:107
  45.2 0.3 copy.118
  45.4 0.3 copy.42
  45.7 0.6 reshape.102
  46.3 2.4 fusion.15
  48.7 1.8 copy.84
  50.6 4.7 %all-to-all-start.1 = ((bf16[64,6,6,256]{3,2,1,0:T(8,128)(2,1)}), bf16[64,6,6,256]{3,2,1,0:T(8,128)(2,1)S(1)}, u32[]{:S(2)}, u32[]{:S(2)}) async-start(bf16[64,6,6,256]{3,2,1,0:T(8,128)(2,1)} %bitcast.17), calls=%async_computation.1 | async-start | bytes 3145728 | tf_op jit(solution)/shard_map/all_to_all | solution.py:114
  55.2 0.9 constant_dynamic-slice_fusion
  56.2 0.2 tile.10
  56.4 0.2 copy.38
  56.6 0.2 copy.39
  56.9 0.1 select_compare_fusion.3
  57.1 21.6 %all-to-all-done.1 = bf16[64,6,6,256]{3,2,1,0:T(8,128)(2,1)S(1)} async-done(((bf16[64,6,6,256]{3,2,1,0:T(8,128)(2,1)}), bf16[64,6,6,256]{3,2,1,0:T(8,128)(2,1)S(1)}, u32[]{:S(2)}, u32[]{:S(2)}) %all-to-all-start.1) | async-done | bytes 1179680 | tf_op jit(solution)/shard_map/all_to_all | solution.py:114
  78.7 0.6 fusion.11
  79.3 0.7 copy.47
  80.0 28.1 %all_to_all.90 = bf16[64,6,6,256]{3,2,1,0:T(8,128)(2,1)S(1)} all-to-all(bf16[64,6,6,256]{3,2,1,0:T(8,128)(2,1)S(1)} %copy.47), channel_id=1, replica_groups=mesh['lat'=8,'lon'=8,'dp'=4] {'lat','lon'}, dimensions={0} | all-to-all | bytes 2359296 | tf_op jit(solution)/shard_map/all_to_all | solution.py:117
  108.1 1.1 convolution_convert_fusion.2
  109.2 2.0 copy.50
  111.1 4.7 %all-to-all-start.3 = ((bf16[1,384,12,128]{3,2,0,1:T(8,128)(2,1)}), bf16[1,384,12,128]{3,2,0,1:T(8,128)(2,1)S(1)}, u32[]{:S(2)}, u32[]{:S(2)}) async-start(bf16[1,384,12,128]{3,2,0,1:T(8,128)(2,1)} %copy.50), calls=%async_computation.3 | async-start | bytes 3145728 | tf_op jit(solution)/shard_map/all_to_all | solution.py:123
  115.8 0.1 broadcast_in_dim.55
  116.0 0.2 mul.95
  116.1 23.2 %all-to-all-done.3 = bf16[1,384,12,128]{3,2,0,1:T(8,128)(2,1)S(1)} async-done(((bf16[1,384,12,128]{3,2,0,1:T(8,128)(2,1)}), bf16[1,384,12,128]{3,2,0,1:T(8,128)(2,1)S(1)}, u32[]{:S(2)}, u32[]{:S(2)}) %all-to-all-start.3) | async-done | bytes 1179680 | tf_op jit(solution)/shard_map/all_to_all | solution.py:123
  139.3 0.4 copy.117
  139.7 0.8 copy.52
  140.5 1.2 reshape.106
  141.7 5.3 %fusion.14 = bf16[1,6,768,128]{3,2,1,0:T(8,128)(2,1)S(1)} fusion(bf16[6,768,128]{2,1,0:T(8,128)(2,1)} %reshape.106, bf16[1,6,768,128]{3,2,1,0:T(8,128)(2,1)} %param.6, bf16[768,768]{1,0:T(8,128)(2,1)} %copy-done.8, bf16[768]{0:T(1024)(128)(2,1)S(1)} %mul.95), kind=kOutput, calls=%fused_computation.34 | convolution fusion | flops 1823735808 | bytes 4720128 | tf_op jit(solution)/shard_map/srnc,kn->srkc/dot_general | solution.py:104
  147.0 0.8 copy.54
  147.8 27.9 %all_to_all.91 = bf16[1,6,768,128]{3,1,0,2:T(8,128)(2,1)S(1)} all-to-all(bf16[1,6,768,128]{3,1,0,2:T(8,128)(2,1)S(1)} %copy.54), channel_id=1, replica_groups=mesh['lat'=8,'lon'=8,'dp'=4] {'lat','lon'}, dimensions={2} | all-to-all | bytes 2359296 | tf_op jit(solution)/shard_map/all_to_all | solution.py:107
  175.7 0.3 copy.116
  176.0 0.3 copy.56
  176.3 2.0 reshape.108
  178.2 2.9 fusion.16
  181.1 1.8 copy.90
  183.0 4.7 %all-to-all-start.5 = ((bf16[64,6,6,256]{3,2,1,0:T(8,128)(2,1)}), bf16[64,6,6,256]{3,2,1,0:T(8,128)(2,1)S(1)}, u32[]{:S(2)}, u32[]{:S(2)}) async-start(bf16[64,6,6,256]{3,2,1,0:T(8,128)(2,1)} %bitcast.35), calls=%async_computation.5 | async-start | bytes 3145728 | tf_op jit(solution)/shard_map/all_to_all | solution.py:114
  187.7 0.2 fusion.63
  187.9 23.2 %all-to-all-done.5 = bf16[64,6,6,256]{3,2,1,0:T(8,128)(2,1)S(1)} async-done(((bf16[64,6,6,256]{3,2,1,0:T(8,128)(2,1)}), bf16[64,6,6,256]{3,2,1,0:T(8,128)(2,1)S(1)}, u32[]{:S(2)}, u32[]{:S(2)}) %all-to-all-start.5) | async-done | bytes 1179680 | tf_op jit(solution)/shard_map/all_to_all | solution.py:114
  211.1 1.1 convolution_bitcast_fusion
  212.3 0.2 convolution_convert_fusion.8
  212.6 0.2 convert_element_type.146
  212.8 0.3 copy.71
  213.0 1.1 convert_element_type.148
  214.1 7.3 %all-to-all-start.8 = ((bf16[4,12,1024]{2,1,0:T(8,128)(2,1)}), bf16[4,12,1024]{2,1,0:T(8,128)(2,1)S(1)}, u32[]{:S(2)}, u32[]{:S(2)}) async-start(bf16[4,12,1024]{2,1,0:T(8,128)(2,1)} %convert_element_type.148), calls=%async_computation.8 | async-start | bytes 262144 | tf_op jit(solution)/shard_map/all_to_all | solution.py:67
  221.4 0.6 fusion.12
  222.0 1.8 copy.61
  223.9 4.9 %all-to-all-done.8 = bf16[4,12,1024]{2,1,0:T(8,128)(2,1)S(1)} async-done(((bf16[4,12,1024]{2,1,0:T(8,128)(2,1)}), bf16[4,12,1024]{2,1,0:T(8,128)(2,1)S(1)}, u32[]{:S(2)}, u32[]{:S(2)}) %all-to-all-start.8) | async-done | bytes 98336 | tf_op jit(solution)/shard_map/all_to_all | solution.py:67
  228.7 6.4 %all-to-all-start.6 = ((bf16[64,6,6,256]{3,2,1,0:T(8,128)(2,1)}), bf16[64,6,6,256]{3,2,1,0:T(8,128)(2,1)S(1)}, u32[]{:S(2)}, u32[]{:S(2)}) async-start(bf16[64,6,6,256]{3,2,1,0:T(8,128)(2,1)} %copy.61), calls=%async_computation.6 | async-start | bytes 3145728 | tf_op jit(solution)/shard_map/all_to_all | solution.py:117
  235.2 23.4 %all-to-all-done.6 = bf16[64,6,6,256]{3,2,1,0:T(8,128)(2,1)S(1)} async-done(((bf16[64,6,6,256]{3,2,1,0:T(8,128)(2,1)}), bf16[64,6,6,256]{3,2,1,0:T(8,128)(2,1)S(1)}, u32[]{:S(2)}, u32[]{:S(2)}) %all-to-all-start.6) | async-done | bytes 1179680 | tf_op jit(solution)/shard_map/all_to_all | solution.py:117
  258.6 1.1 broadcast_in_dim.58
  259.7 3.8 %all-to-all-start.9 = ((bf16[32,12,1024]{2,1,0:T(8,128)(2,1)}), bf16[32,12,1024]{2,1,0:T(8,128)(2,1)S(1)}, u32[]{:S(2)}, u32[]{:S(2)}) async-start(bf16[32,12,1024]{2,1,0:T(8,128)(2,1)} %broadcast_in_dim.58), calls=%async_computation.9 | async-start | bytes 2097152 | tf_op jit(solution)/shard_map/all_to_all | solution.py:70
  263.6 3.5 %convolution_convert_fusion = bf16[6,384,256]{1,2,0:T(8,128)(2,1)} fusion(bf16[384,6,256]{2,1,0:T(8,128)(2,1)S(1)} %bitcast.126, bf16[6,384,384]{2,1,0:T(8,128)(2,1)} %param.7, pred[6,384]{1,0:T(8,128)(4,1)S(1)} %iota_compare_fusion), kind=kOutput, calls=%fused_computation.21 | convolution fusion | flops 454459392 | bytes 4131072 | tf_op jit(solution)/shard_map/slmc,mal->samc/dot_general | solution.py:119
  267.1 2.9 copy.64
  270.0 21.9 %all-to-all-done.9 = bf16[32,12,1024]{2,1,0:T(8,128)(2,1)S(1)} async-done(((bf16[32,12,1024]{2,1,0:T(8,128)(2,1)}), bf16[32,12,1024]{2,1,0:T(8,128)(2,1)S(1)}, u32[]{:S(2)}, u32[]{:S(2)}) %all-to-all-start.9) | async-done | bytes 786464 | tf_op jit(solution)/shard_map/all_to_all | solution.py:70
  292.0 6.5 %all-to-all-start.7 = ((bf16[1,384,12,128]{3,2,0,1:T(8,128)(2,1)}), bf16[1,384,12,128]{3,2,0,1:T(8,128)(2,1)S(1)}, u32[]{:S(2)}, u32[]{:S(2)}) async-start(bf16[1,384,12,128]{3,2,0,1:T(8,128)(2,1)} %copy.64), calls=%async_computation.7 | async-start | bytes 3145728 | tf_op jit(solution)/shard_map/all_to_all | solution.py:123
  298.5 1.8 reshape.113
  300.3 21.7 %all-to-all-done.7 = bf16[1,384,12,128]{3,2,0,1:T(8,128)(2,1)S(1)} async-done(((bf16[1,384,12,128]{3,2,0,1:T(8,128)(2,1)}), bf16[1,384,12,128]{3,2,0,1:T(8,128)(2,1)S(1)}, u32[]{:S(2)}, u32[]{:S(2)}) %all-to-all-start.7) | async-done | bytes 1179680 | tf_op jit(solution)/shard_map/all_to_all | solution.py:123
  322.0 0.4 copy.115
  322.4 0.8 copy.66
  323.2 0.3 reshape.112
  323.5 3.9 %fusion.1 = bf16[1,6,768,128]{3,2,1,0:T(8,128)(2,1)} fusion(bf16[1,6,768,128]{3,2,1,0:T(8,128)(2,1)} %param.6, bf16[6,768,128]{2,1,0:T(8,128)(2,1)S(1)} %reshape.112, bf16[768,768]{1,0:T(8,128)(2,1)} %copy-done.8), kind=kOutput, calls=%fused_computation.4 | convolution fusion | flops 907739136 | bytes 4718592 | tf_op jit(solution)/shard_map/srkc,kn->srnc/dot_general | solution.py:124
  (40 shorter events, 0.5 us)
Async XLA Ops:
  0.6 7.5 %copy-start = (bf16[1,6,768,128]{3,2,1,0:T(8,128)(2,1)S(1)}, bf16[1,6,768,128]{3,2,1,0:T(8,128)(2,1)}, u32[]{:S(2)}) copy-start(bf16[1,6,768,128]{3,2,1,0:T(8,128)(2,1)} %param.5) | copy-start | bytes 3538948
  8.1 1.1 copy-start.8
  11.2 10.5 %copy-start.6 = (s32[384]{0:T(512)S(1)}, s32[384]{0:T(512)}, u32[]{:S(2)}) copy-start(s32[384]{0:T(512)} %param.8) | copy-start | bytes 4612
  11.2 34.0 %all-to-all-start = ((bf16[1,6,768,128]{3,1,0,2:T(8,128)(2,1)}), bf16[1,6,768,128]{3,1,0,2:T(8,128)(2,1)S(1)}, u32[]{:S(2)}, u32[]{:S(2)}) async-start(bf16[1,6,768,128]{3,1,0,2:T(8,128)(2,1)} %copy.40), calls=%async_computation | async-start | bytes 3145728 | tf_op jit(solution)/shard_map/all_to_all | solution.py:107
  50.6 28.2 %all-to-all-start.1 = ((bf16[64,6,6,256]{3,2,1,0:T(8,128)(2,1)}), bf16[64,6,6,256]{3,2,1,0:T(8,128)(2,1)S(1)}, u32[]{:S(2)}, u32[]{:S(2)}) async-start(bf16[64,6,6,256]{3,2,1,0:T(8,128)(2,1)} %bitcast.17), calls=%async_computation.1 | async-start | bytes 3145728 | tf_op jit(solution)/shard_map/all_to_all | solution.py:114
  57.1 22.2 %copy-start.2 = (bf16[6,128,128]{2,1,0:T(8,128)(2,1)}, bf16[6,128,128]{2,1,0:T(8,128)(2,1)S(1)}, u32[]{:S(2)}) copy-start(bf16[6,128,128]{2,1,0:T(8,128)(2,1)S(1)} %get-tuple-element.4) | copy-start | bytes 589828
  57.1 22.2 %copy-start.4 = (bf16[6,128,128]{2,1,0:T(8,128)(2,1)}, bf16[6,128,128]{2,1,0:T(8,128)(2,1)S(1)}, u32[]{:S(2)}) copy-start(bf16[6,128,128]{2,1,0:T(8,128)(2,1)S(1)} %get-tuple-element.5) | copy-start | bytes 589828
  80.0 28.1 %copy-start.7 = (bf16[6,384,384]{2,1,0:T(8,128)(2,1)S(1)}, bf16[6,384,384]{2,1,0:T(8,128)(2,1)}, u32[]{:S(2)}) copy-start(bf16[6,384,384]{2,1,0:T(8,128)(2,1)} %param.7) | copy-start | bytes 5308420
  111.1 28.2 %all-to-all-start.3 = ((bf16[1,384,12,128]{3,2,0,1:T(8,128)(2,1)}), bf16[1,384,12,128]{3,2,0,1:T(8,128)(2,1)S(1)}, u32[]{:S(2)}, u32[]{:S(2)}) async-start(bf16[1,384,12,128]{3,2,0,1:T(8,128)(2,1)} %copy.50), calls=%async_computation.3 | async-start | bytes 3145728 | tf_op jit(solution)/shard_map/all_to_all | solution.py:123
  183.0 28.2 %all-to-all-start.5 = ((bf16[64,6,6,256]{3,2,1,0:T(8,128)(2,1)}), bf16[64,6,6,256]{3,2,1,0:T(8,128)(2,1)S(1)}, u32[]{:S(2)}, u32[]{:S(2)}) async-start(bf16[64,6,6,256]{3,2,1,0:T(8,128)(2,1)} %bitcast.35), calls=%async_computation.5 | async-start | bytes 3145728 | tf_op jit(solution)/shard_map/all_to_all | solution.py:114
  212.3 9.1 %copy-start.3 = (bf16[6,128,128]{2,1,0:T(8,128)(2,1)S(1)}, bf16[6,128,128]{2,1,0:T(8,128)(2,1)}, u32[]{:S(2)}) copy-start(bf16[6,128,128]{2,1,0:T(8,128)(2,1)} %copy-done.2) | copy-start | bytes 589828
  212.3 9.1 %copy-start.5 = (bf16[6,128,128]{2,1,0:T(8,128)(2,1)S(1)}, bf16[6,128,128]{2,1,0:T(8,128)(2,1)}, u32[]{:S(2)}) copy-start(bf16[6,128,128]{2,1,0:T(8,128)(2,1)} %copy-done.4) | copy-start | bytes 589828
  214.1 14.6 %all-to-all-start.8 = ((bf16[4,12,1024]{2,1,0:T(8,128)(2,1)}), bf16[4,12,1024]{2,1,0:T(8,128)(2,1)S(1)}, u32[]{:S(2)}, u32[]{:S(2)}) async-start(bf16[4,12,1024]{2,1,0:T(8,128)(2,1)} %convert_element_type.148), calls=%async_computation.8 | async-start | bytes 262144 | tf_op jit(solution)/shard_map/all_to_all | solution.py:67
  228.7 29.9 %all-to-all-start.6 = ((bf16[64,6,6,256]{3,2,1,0:T(8,128)(2,1)}), bf16[64,6,6,256]{3,2,1,0:T(8,128)(2,1)S(1)}, u32[]{:S(2)}, u32[]{:S(2)}) async-start(bf16[64,6,6,256]{3,2,1,0:T(8,128)(2,1)} %copy.61), calls=%async_computation.6 | async-start | bytes 3145728 | tf_op jit(solution)/shard_map/all_to_all | solution.py:117
  259.7 32.2 %all-to-all-start.9 = ((bf16[32,12,1024]{2,1,0:T(8,128)(2,1)}), bf16[32,12,1024]{2,1,0:T(8,128)(2,1)S(1)}, u32[]{:S(2)}, u32[]{:S(2)}) async-start(bf16[32,12,1024]{2,1,0:T(8,128)(2,1)} %broadcast_in_dim.58), calls=%async_computation.9 | async-start | bytes 2097152 | tf_op jit(solution)/shard_map/all_to_all | solution.py:70
  292.0 30.0 %all-to-all-start.7 = ((bf16[1,384,12,128]{3,2,0,1:T(8,128)(2,1)}), bf16[1,384,12,128]{3,2,0,1:T(8,128)(2,1)S(1)}, u32[]{:S(2)}, u32[]{:S(2)}) async-start(bf16[1,384,12,128]{3,2,0,1:T(8,128)(2,1)} %copy.64), calls=%async_computation.7 | async-start | bytes 3145728 | tf_op jit(solution)/shard_map/all_to_all | solution.py:123
  323.5 3.9 %copy-start.1 = (bf16[1,6,768,128]{3,2,1,0:T(8,128)(2,1)S(1)}, bf16[1,6,768,128]{3,2,1,0:T(8,128)(2,1)}, u32[]{:S(2)}) copy-start(bf16[1,6,768,128]{3,2,1,0:T(8,128)(2,1)} %param.5) | copy-start | bytes 3538948
where the time goes:
time: 329 us; the launch traced here: 327 us
  waiting for transfers between devices  163 us (50%)
  blocking collectives  56 us (17%)
  starting transfers between devices  48.5 us (15%)
  local copies, waits for them, and re-layouts  27.8 us (8%)
  matrix products  23.8 us (7%)
  other arithmetic  6.89 us (2%)
    all_to_all x2, waiting for transfers between devices, synthesize(): lax.all_to_all(spectra, ('lat', 'lon'), split_axis=1, concat_axis=2, tile...  44.9 us
    all_to_all x2, waiting for transfers between devices, analyze(): lax.all_to_all(spectral, ('lat', 'lon'), split_axis=0, concat_axis=0, til...  44.7 us
    all_to_all x1, blocking collectives, synthesize(): lax.all_to_all(spectral, ('lat', 'lon'), split_axis=0, concat_axis=0, til...  28.1 us
    all_to_all x1, blocking collectives, analyze(): lax.all_to_all(spectra, ('lat', 'lon'), split_axis=2, concat_axis=1, tile...  27.9 us
    all_to_all x1, waiting for transfers between devices, synthesize(): lax.all_to_all(spectral, ('lat', 'lon'), split_axis=0, concat_axis=0, til...  23.4 us
    all_to_all x1, waiting for transfers between devices, analyze(): lax.all_to_all(spectra, ('lat', 'lon'), split_axis=2, concat_axis=1, tile...  23.3 us
    all_to_all x1, waiting for transfers between devices, gather_sum(): lax.all_to_all(tiled, gather_axes, split_axis=0, concat_axis=0, tiled=True)  21.9 us
    all_to_all x2, starting transfers between devices, synthesize(): lax.all_to_all(spectra, ('lat', 'lon'), split_axis=1, concat_axis=2, tile...  11.2 us
  transfers between devices with their start and end apart: 8, of which 8 were waited for; matrix products, arithmetic and copies ran while one was open for 4% of the time, Pallas kernels for 0%

commit v1 on v0

--- a/solution.py
+++ b/solution.py
@@ -55,6 +55,19 @@
     normal_cdf = 0.5 * (1.0 + lax.erf(branch * (1.0 / math.sqrt(2.0))))
     density = jnp.exp(-0.5 * branch * branch) * (1.0 / math.sqrt(2.0 * math.pi))
     return normal_cdf + branch * density
+
+
+def gather_after_sum(values, sum_axis, gather_axes):
+    count = 1
+    for name in gather_axes:
+        count *= lax.axis_size(name)
+    parts = lax.axis_size(sum_axis)
+    rows = lax.psum(values, sum_axis).reshape(-1, values.shape[-1])
+    own = rows.reshape(parts, rows.shape[0] // parts, rows.shape[1])
+    mine = lax.dynamic_index_in_dim(own, lax.axis_index(sum_axis), 0, keepdims=False)
+    tiled = jnp.broadcast_to(mine[None], (count,) + mine.shape)
+    gathered = lax.all_to_all(tiled, gather_axes, split_axis=0, concat_axis=0, tiled=True)
+    return gathered.reshape(-1, values.shape[-1])
 
 
 def gather_sum(values, sum_axis, gather_axes):
@@ -164,7 +177,7 @@
         .transpose(0, 3, 1, 2, 4)
         .reshape(held_weights.shape)
     )
-    weight_grad = gather_sum(local_grad.astype(jnp.bfloat16), "dp", ("lon", "dp"))
+    weight_grad = gather_after_sum(local_grad.astype(jnp.bfloat16), "dp", ("lon", "dp"))
     weight_grad = weight_grad.reshape(weights.shape).astype(jnp.float32)
     demixed_rows = jnp.einsum(
         "slmd,lcd->slmc", back_rows, mixing, preferred_element_type=jnp.float32

time: 329 us -> 362 us (1.10)
  blocking collectives: 56 us -> 84.1 us
  between operations: 1.14 us -> 14.5 us
  starting transfers between devices: 48.5 us -> 41.8 us
    psum x0 -> x1, waiting for transfers between devices: none -> 50.3 us  [gather_after_sum(): rows = lax.psum(values, sum_axis).reshape(-1, values.shape[-1])]
    all_to_all x0 -> x1, blocking collectives: none -> 28.1 us  [analyze(): lax.all_to_all(spectral, ('lat', 'lon'), split_axis=0, concat_axis=0, til...]
    all_to_all x1, waiting for transfers between devices: 23.4 us -> 0.01 us  [synthesize(): lax.all_to_all(spectral, ('lat', 'lon'), split_axis=0, concat_axis=0, til...]
    all_to_all x2 -> x1, waiting for transfers between devices: 44.7 us -> 21.6 us  [analyze(): lax.all_to_all(spectral, ('lat', 'lon'), split_axis=0, concat_axis=0, til...]
    all_to_all x2 -> x1, starting transfers between devices: 9.35 us -> 4.67 us  [analyze(): lax.all_to_all(spectral, ('lat', 'lon'), split_axis=0, concat_axis=0, til...]
    all_to_all x2 -> x1, waiting for transfers between devices: 26.8 us -> 23.7 us  [gather_after_sum(): lax.all_to_all(tiled, gather_axes, split_axis=0, concat_axis=0, tiled=True)]
    all_to_all x2 -> x1, starting transfers between devices: 11.1 us -> 9.67 us  [gather_after_sum(): lax.all_to_all(tiled, gather_axes, split_axis=0, concat_axis=0, tiled=True)]
  transfers between devices with their start and end apart: 8 -> 7, of which waited for: 8 -> 6; matrix products, arithmetic and copies ran while one was open for 4% -> 4% of each run, Pallas kernels for 0% -> 0%
where the time goes in v1:
time: 362 us; the launch traced here: 361 us
  waiting for transfers between devices  164 us (45%)
  blocking collectives  84.1 us (23%)
  starting transfers between devices  41.8 us (12%)
  local copies, waits for them, and re-layouts  26.5 us (7%)
  matrix products  23.3 us (6%)
  between operations  14.5 us (4%)
  other arithmetic  6.86 us (2%)
    psum x1, waiting for transfers between devices, gather_after_sum(): rows = lax.psum(values, sum_axis).reshape(-1, values.shape[-1])  50.3 us
    all_to_all x2, waiting for transfers between devices, synthesize(): lax.all_to_all(spectra, ('lat', 'lon'), split_axis=1, concat_axis=2, tile...  44.9 us
    all_to_all x1, blocking collectives, synthesize(): lax.all_to_all(spectral, ('lat', 'lon'), split_axis=0, concat_axis=0, til...  28.1 us
    all_to_all x1, blocking collectives, analyze(): lax.all_to_all(spectral, ('lat', 'lon'), split_axis=0, concat_axis=0, til...  28.1 us
    all_to_all x1, blocking collectives, analyze(): lax.all_to_all(spectra, ('lat', 'lon'), split_axis=2, concat_axis=1, tile...  28 us
    all_to_all x1, waiting for transfers between devices, gather_after_sum(): lax.all_to_all(tiled, gather_axes, split_axis=0, concat_axis=0, tiled=True)  23.7 us
    all_to_all x1, waiting for transfers between devices, analyze(): lax.all_to_all(spectra, ('lat', 'lon'), split_axis=2, concat_axis=1, tile...  23.3 us
    all_to_all x1, waiting for transfers between devices, analyze(): lax.all_to_all(spectral, ('lat', 'lon'), split_axis=0, concat_axis=0, til...  21.6 us
  transfers between devices with their start and end apart: 7, of which 6 were waited for; matrix products, arithmetic and copies ran while one was open for 4% of the time, Pallas kernels for 0%

profile of v1, /device:TPU:1, one launch (start us, length us, event | category | flops | bytes accessed | tf_op | source)
XLA Modules:
  0.0 360.8 jit_solution(5588633993922279368)
XLA Ops:
  7.2 6.3 %multiply_convert_fusion.1 = (bf16[384,768]{1,0:T(8,128)(2,1)S(1)}, bf16[384,768]{1,0:T(8,128)(2,1)S(1)}) fusion(s32[384]{0:T(512)} %param.8), kind=kLoop, calls=%fused_computation.53 | loop fusion | flops 4128768 | bytes 1181184 | tf_op jit(solution)/shard_map/convert_element_type | solution.py:20
  13.5 1.2 fusion.10
  14.7 1.1 fusion.13
  15.8 2.0 copy.40
  17.8 10.5 %all-to-all-start = ((bf16[1,6,768,128]{3,1,0,2:T(8,128)(2,1)}), bf16[1,6,768,128]{3,1,0,2:T(8,128)(2,1)S(1)}, u32[]{:S(2)}, u32[]{:S(2)}) async-start(bf16[1,6,768,128]{3,1,0,2:T(8,128)(2,1)} %copy.40), calls=%async_computation | async-start | bytes 3145728 | tf_op jit(solution)/shard_map/all_to_all | solution.py:120
  28.3 0.1 dynamic_slice.10
  28.4 23.3 %all-to-all-done = bf16[1,6,768,128]{3,1,0,2:T(8,128)(2,1)S(1)} async-done(((bf16[1,6,768,128]{3,1,0,2:T(8,128)(2,1)}), bf16[1,6,768,128]{3,1,0,2:T(8,128)(2,1)S(1)}, u32[]{:S(2)}, u32[]{:S(2)}) %all-to-all-start) | async-done | bytes 1179680 | tf_op jit(solution)/shard_map/all_to_all | solution.py:120
  51.7 0.3 copy.118
  52.0 0.3 copy.42
  52.3 0.6 reshape.100
  52.8 2.4 fusion.15
  55.3 1.8 copy.84
  57.1 4.7 %all-to-all-start.1 = ((bf16[64,6,6,256]{3,2,1,0:T(8,128)(2,1)}), bf16[64,6,6,256]{3,2,1,0:T(8,128)(2,1)S(1)}, u32[]{:S(2)}, u32[]{:S(2)}) async-start(bf16[64,6,6,256]{3,2,1,0:T(8,128)(2,1)} %bitcast.17), calls=%async_computation.1 | async-start | bytes 3145728 | tf_op jit(solution)/shard_map/all_to_all | solution.py:127
  61.8 0.9 constant_dynamic-slice_fusion
  62.7 0.2 tile.10
  62.9 0.2 copy.38
  63.2 0.2 copy.39
  63.4 0.1 select_compare_fusion.3
  63.7 21.6 %all-to-all-done.1 = bf16[64,6,6,256]{3,2,1,0:T(8,128)(2,1)S(1)} async-done(((bf16[64,6,6,256]{3,2,1,0:T(8,128)(2,1)}), bf16[64,6,6,256]{3,2,1,0:T(8,128)(2,1)S(1)}, u32[]{:S(2)}, u32[]{:S(2)}) %all-to-all-start.1) | async-done | bytes 1179680 | tf_op jit(solution)/shard_map/all_to_all | solution.py:127
  85.3 0.6 fusion.11
  85.8 0.7 copy.47
  86.6 28.1 %all_to_all.85 = bf16[64,6,6,256]{3,2,1,0:T(8,128)(2,1)S(1)} all-to-all(bf16[64,6,6,256]{3,2,1,0:T(8,128)(2,1)S(1)} %copy.47), channel_id=1, replica_groups=mesh['lat'=8,'lon'=8,'dp'=4] {'lat','lon'}, dimensions={0} | all-to-all | bytes 2359296 | tf_op jit(solution)/shard_map/all_to_all | solution.py:130
  114.6 1.1 convolution_convert_fusion.2
  115.7 2.0 copy.50
  117.7 4.7 %all-to-all-start.3 = ((bf16[1,384,12,128]{3,2,0,1:T(8,128)(2,1)}), bf16[1,384,12,128]{3,2,0,1:T(8,128)(2,1)S(1)}, u32[]{:S(2)}, u32[]{:S(2)}) async-start(bf16[1,384,12,128]{3,2,0,1:T(8,128)(2,1)} %copy.50), calls=%async_computation.3 | async-start | bytes 3145728 | tf_op jit(solution)/shard_map/all_to_all | solution.py:136
  122.4 0.1 broadcast_in_dim.57
  122.5 0.2 mul.95
  122.7 23.2 %all-to-all-done.3 = bf16[1,384,12,128]{3,2,0,1:T(8,128)(2,1)S(1)} async-done(((bf16[1,384,12,128]{3,2,0,1:T(8,128)(2,1)}), bf16[1,384,12,128]{3,2,0,1:T(8,128)(2,1)S(1)}, u32[]{:S(2)}, u32[]{:S(2)}) %all-to-all-start.3) | async-done | bytes 1179680 | tf_op jit(solution)/shard_map/all_to_all | solution.py:136
  145.8 0.4 copy.117
  146.2 0.8 copy.52
  147.1 1.2 reshape.104
  148.2 5.3 %fusion.14 = bf16[1,6,768,128]{3,2,1,0:T(8,128)(2,1)S(1)} fusion(bf16[6,768,128]{2,1,0:T(8,128)(2,1)} %reshape.104, bf16[1,6,768,128]{3,2,1,0:T(8,128)(2,1)} %param.6, bf16[768,768]{1,0:T(8,128)(2,1)} %copy-done.8, bf16[768]{0:T(1024)(128)(2,1)S(1)} %mul.95), kind=kOutput, calls=%fused_computation.34 | convolution fusion | flops 1823735808 | bytes 4720128 | tf_op jit(solution)/shard_map/srnc,kn->srkc/dot_general | solution.py:117
  153.5 0.8 copy.54
  154.3 28.0 %all_to_all.86 = bf16[1,6,768,128]{3,1,0,2:T(8,128)(2,1)S(1)} all-to-all(bf16[1,6,768,128]{3,1,0,2:T(8,128)(2,1)S(1)} %copy.54), channel_id=1, replica_groups=mesh['lat'=8,'lon'=8,'dp'=4] {'lat','lon'}, dimensions={2} | all-to-all | bytes 2359296 | tf_op jit(solution)/shard_map/all_to_all | solution.py:120
  182.3 0.3 copy.116
  182.5 0.3 copy.56
  182.8 2.0 reshape.106
  184.8 2.9 fusion.16
  187.7 0.7 copy.90
  188.4 28.1 %all_to_all.87 = bf16[64,6,6,256]{3,2,1,0:T(8,128)(2,1)S(1)} all-to-all(bf16[64,6,6,256]{3,2,1,0:T(8,128)(2,1)S(1)} %bitcast.128), channel_id=1, replica_groups=mesh['lat'=8,'lon'=8,'dp'=4] {'lat','lon'}, dimensions={0} | all-to-all | bytes 2359296 | tf_op jit(solution)/shard_map/all_to_all | solution.py:127
  216.5 0.6 fusion.12
  217.1 1.8 copy.61
  218.9 5.1 %all-to-all-start.6 = ((bf16[64,6,6,256]{3,2,1,0:T(8,128)(2,1)}), bf16[64,6,6,256]{3,2,1,0:T(8,128)(2,1)}, u32[]{:S(2)}, u32[]{:S(2)}) async-start(bf16[64,6,6,256]{3,2,1,0:T(8,128)(2,1)} %copy.61), calls=%async_computation.6 | async-start | bytes 3145728 | tf_op jit(solution)/shard_map/all_to_all | solution.py:130
  224.2 0.2 fusion.63
  224.4 1.1 convolution_bitcast_fusion
  225.5 0.1 fusion.57
  225.6 0.3 convolution_convert_fusion.8
  225.8 0.2 convert_element_type.143
  226.0 0.3 copy.71
  226.3 1.1 reshape_reshape.4
  227.4 50.3 %all-reduce.2.cloned.1.call-done = bf16[4,12,1024]{2,1,0:T(8,128)(2,1)} async-done(((bf16[4,12,1024]{2,1,0:T(8,128)(2,1)}), bf16[4,12,1024]{2,1,0:T(8,128)(2,1)}) %all-reduce.2.cloned.1.call-update) | async-done | bytes 98320 | tf_op jit(solution)/shard_map/psum | solution.py:65
  277.7 0.8 dynamic-slice_bitcast_fusion
  278.5 1.1 broadcast_in_dim.61
  279.6 9.7 %all-to-all-start.8 = ((bf16[32,12,1024]{2,1,0:T(8,128)(2,1)}), bf16[32,12,1024]{2,1,0:T(8,128)(2,1)S(1)}, u32[]{:S(2)}, u32[]{:S(2)}) async-start(bf16[32,12,1024]{2,1,0:T(8,128)(2,1)} %broadcast_in_dim.61), calls=%async_computation.8 | async-start | bytes 2097152 | tf_op jit(solution)/shard_map/all_to_all | solution.py:69
  289.3 3.0 convolution_convert_fusion
  292.2 2.0 copy.64
  294.3 23.7 %all-to-all-done.8 = bf16[32,12,1024]{2,1,0:T(8,128)(2,1)S(1)} async-done(((bf16[32,12,1024]{2,1,0:T(8,128)(2,1)}), bf16[32,12,1024]{2,1,0:T(8,128)(2,1)S(1)}, u32[]{:S(2)}, u32[]{:S(2)}) %all-to-all-start.8) | async-done | bytes 786464 | tf_op jit(solution)/shard_map/all_to_all | solution.py:69
  317.9 7.1 %all-to-all-start.7 = ((bf16[1,384,12,128]{3,2,0,1:T(8,128)(2,1)}), bf16[1,384,12,128]{3,2,0,1:T(8,128)(2,1)S(1)}, u32[]{:S(2)}, u32[]{:S(2)}) async-start(bf16[1,384,12,128]{3,2,0,1:T(8,128)(2,1)} %copy.64), calls=%async_computation.7 | async-start | bytes 3145728 | tf_op jit(solution)/shard_map/all_to_all | solution.py:136
  325.0 1.8 reshape.112
  326.8 21.7 %all-to-all-done.7 = bf16[1,384,12,128]{3,2,0,1:T(8,128)(2,1)S(1)} async-done(((bf16[1,384,12,128]{3,2,0,1:T(8,128)(2,1)}), bf16[1,384,12,128]{3,2,0,1:T(8,128)(2,1)S(1)}, u32[]{:S(2)}, u32[]{:S(2)}) %all-to-all-start.7) | async-done | bytes 1179680 | tf_op jit(solution)/shard_map/all_to_all | solution.py:136
  348.5 0.4 copy.115
  348.9 0.8 copy.66
  349.7 0.3 reshape.110
  350.1 3.9 %fusion.1 = bf16[1,6,768,128]{3,2,1,0:T(8,128)(2,1)} fusion(bf16[1,6,768,128]{3,2,1,0:T(8,128)(2,1)} %param.6, bf16[6,768,128]{2,1,0:T(8,128)(2,1)S(1)} %reshape.110, bf16[768,768]{1,0:T(8,128)(2,1)} %copy-done.8), kind=kOutput, calls=%fused_computation.4 | convolution fusion | flops 907739136 | bytes 4718592 | tf_op jit(solution)/shard_map/srkc,kn->srnc/dot_general | solution.py:137
  (40 shorter events, 0.4 us)
Async XLA Ops:
  7.2 7.5 %copy-start = (bf16[1,6,768,128]{3,2,1,0:T(8,128)(2,1)S(1)}, bf16[1,6,768,128]{3,2,1,0:T(8,128)(2,1)}, u32[]{:S(2)}) copy-start(bf16[1,6,768,128]{3,2,1,0:T(8,128)(2,1)} %param.5) | copy-start | bytes 3538948
  14.7 1.1 copy-start.8
  17.8 10.5 %copy-start.6 = (s32[384]{0:T(512)S(1)}, s32[384]{0:T(512)}, u32[]{:S(2)}) copy-start(s32[384]{0:T(512)} %param.8) | copy-start | bytes 4612
  17.8 34.0 %all-to-all-start = ((bf16[1,6,768,128]{3,1,0,2:T(8,128)(2,1)}), bf16[1,6,768,128]{3,1,0,2:T(8,128)(2,1)S(1)}, u32[]{:S(2)}, u32[]{:S(2)}) async-start(bf16[1,6,768,128]{3,1,0,2:T(8,128)(2,1)} %copy.40), calls=%async_computation | async-start | bytes 3145728 | tf_op jit(solution)/shard_map/all_to_all | solution.py:120
  57.1 28.2 %all-to-all-start.1 = ((bf16[64,6,6,256]{3,2,1,0:T(8,128)(2,1)}), bf16[64,6,6,256]{3,2,1,0:T(8,128)(2,1)S(1)}, u32[]{:S(2)}, u32[]{:S(2)}) async-start(bf16[64,6,6,256]{3,2,1,0:T(8,128)(2,1)} %bitcast.17), calls=%async_computation.1 | async-start | bytes 3145728 | tf_op jit(solution)/shard_map/all_to_all | solution.py:127
  63.7 22.2 %copy-start.2 = (bf16[6,128,128]{2,1,0:T(8,128)(2,1)}, bf16[6,128,128]{2,1,0:T(8,128)(2,1)S(1)}, u32[]{:S(2)}) copy-start(bf16[6,128,128]{2,1,0:T(8,128)(2,1)S(1)} %get-tuple-element.4) | copy-start | bytes 589828
  63.7 22.2 %copy-start.4 = (bf16[6,128,128]{2,1,0:T(8,128)(2,1)}, bf16[6,128,128]{2,1,0:T(8,128)(2,1)S(1)}, u32[]{:S(2)}) copy-start(bf16[6,128,128]{2,1,0:T(8,128)(2,1)S(1)} %get-tuple-element.5) | copy-start | bytes 589828
  86.5 28.1 %copy-start.7 = (bf16[6,384,384]{2,1,0:T(8,128)(2,1)S(1)}, bf16[6,384,384]{2,1,0:T(8,128)(2,1)}, u32[]{:S(2)}) copy-start(bf16[6,384,384]{2,1,0:T(8,128)(2,1)} %param.7) | copy-start | bytes 5308420
  117.7 28.2 %all-to-all-start.3 = ((bf16[1,384,12,128]{3,2,0,1:T(8,128)(2,1)}), bf16[1,384,12,128]{3,2,0,1:T(8,128)(2,1)S(1)}, u32[]{:S(2)}, u32[]{:S(2)}) async-start(bf16[1,384,12,128]{3,2,0,1:T(8,128)(2,1)} %copy.50), calls=%async_computation.3 | async-start | bytes 3145728 | tf_op jit(solution)/shard_map/all_to_all | solution.py:136
  188.4 28.1 %copy-start.3 = (bf16[6,128,128]{2,1,0:T(8,128)(2,1)S(1)}, bf16[6,128,128]{2,1,0:T(8,128)(2,1)}, u32[]{:S(2)}) copy-start(bf16[6,128,128]{2,1,0:T(8,128)(2,1)} %copy-done.2) | copy-start | bytes 589828
  188.4 28.1 %copy-start.5 = (bf16[6,128,128]{2,1,0:T(8,128)(2,1)S(1)}, bf16[6,128,128]{2,1,0:T(8,128)(2,1)}, u32[]{:S(2)}) copy-start(bf16[6,128,128]{2,1,0:T(8,128)(2,1)} %copy-done.4) | copy-start | bytes 589828
  218.9 59.6 %all-to-all-start.6 = ((bf16[64,6,6,256]{3,2,1,0:T(8,128)(2,1)}), bf16[64,6,6,256]{3,2,1,0:T(8,128)(2,1)}, u32[]{:S(2)}, u32[]{:S(2)}) async-start(bf16[64,6,6,256]{3,2,1,0:T(8,128)(2,1)} %copy.61), calls=%async_computation.6 | async-start | bytes 3145728 | tf_op jit(solution)/shard_map/all_to_all | solution.py:130
  224.0 53.7 %all-reduce.2.cloned.1.call-start = ((), (), s32[]{:S(2)}) async-start(), calls=%async_computation.9 | async-start | bytes 262144 | tf_op jit(solution)/shard_map/psum | solution.py:65
  279.6 38.3 %all-to-all-start.8 = ((bf16[32,12,1024]{2,1,0:T(8,128)(2,1)}), bf16[32,12,1024]{2,1,0:T(8,128)(2,1)S(1)}, u32[]{:S(2)}, u32[]{:S(2)}) async-start(bf16[32,12,1024]{2,1,0:T(8,128)(2,1)} %broadcast_in_dim.61), calls=%async_computation.8 | async-start | bytes 2097152 | tf_op jit(solution)/shard_map/all_to_all | solution.py:69
  317.9 30.6 %all-to-all-start.7 = ((bf16[1,384,12,128]{3,2,0,1:T(8,128)(2,1)}), bf16[1,384,12,128]{3,2,0,1:T(8,128)(2,1)S(1)}, u32[]{:S(2)}, u32[]{:S(2)}) async-start(bf16[1,384,12,128]{3,2,0,1:T(8,128)(2,1)} %copy.64), calls=%async_computation.7 | async-start | bytes 3145728 | tf_op jit(solution)/shard_map/all_to_all | solution.py:136
  350.1 3.9 %copy-start.1 = (bf16[1,6,768,128]{3,2,1,0:T(8,128)(2,1)S(1)}, bf16[1,6,768,128]{3,2,1,0:T(8,128)(2,1)}, u32[]{:S(2)}) copy-start(bf16[1,6,768,128]{3,2,1,0:T(8,128)(2,1)} %param.5) | copy-start | bytes 3538948
Sparse Core Ops, SparseCore 0:
  228.1 49.6 all-reduce.1

commit v2 on v0

--- a/solution.py
+++ b/solution.py
@@ -14,11 +14,13 @@
     slots = wave_ids.shape[0]
     columns = jnp.arange(NLON, dtype=jnp.int32)
     phase_int = wave_ids[:, None] * columns[None, :] % NLON
-    angles = phase_int.astype(jnp.float32) * jnp.float32(2.0 * math.pi / NLON)
+    angles = columns.astype(jnp.float32) * jnp.float32(2.0 * math.pi / NLON)
     factor = jnp.float32(1.0 / math.sqrt(NLON))
-    parts = jnp.concatenate(
-        [(jnp.cos(angles) * factor).astype(jnp.bfloat16), (-jnp.sin(angles) * factor).astype(jnp.bfloat16)],
-        axis=0,
+    lookup = jnp.concatenate(
+        [(jnp.cos(angles) * factor).astype(jnp.bfloat16), (-jnp.sin(angles) * factor).astype(jnp.bfloat16)]
+    )
+    parts = jnp.take(
+        lookup, jnp.concatenate([phase_int, phase_int + NLON], axis=0), mode="clip"
     )
     table_row = lax.broadcasted_iota(jnp.int32, (2 * slots, 2 * slots), 0)
     part_row = lax.broadcasted_iota(jnp.int32, (2 * slots, 2 * slots), 1)

time: 329 us -> 6560 us (19.94)
  local copies, waits for them, and re-layouts: 27.8 us -> 6250 us
    gather x0 -> x2, local copies, waits for them, and re-layouts: none -> 6210 us  [build_tables(): jnp.take(lookup, jnp.concatenate([phase_int, phase_int + NLON], axis=0),...]
  transfers between devices with their start and end apart: 8 -> 8, of which waited for: 8 -> 8; matrix products, arithmetic and copies ran while one was open for 4% -> 0% of each run, Pallas kernels for 0% -> 0%
where the time goes in v2:
time: 6560 us; the launch traced here: 6550 us
  local copies, waits for them, and re-layouts  6250 us (95%)
  waiting for transfers between devices  161 us (2%)
    gather x2, local copies, waits for them, and re-layouts, build_tables(): jnp.take(lookup, jnp.concatenate([phase_int, phase_int + NLON], axis=0),...  6210 us
  transfers between devices with their start and end apart: 8, of which 8 were waited for; matrix products, arithmetic and copies ran while one was open for 0% of the time, Pallas kernels for 0%

profile of v2, /device:TPU:1, one launch (start us, length us, event | category | flops | bytes accessed | tf_op | source)
XLA Modules:
  0.0 6549.1 jit_solution(15067022452052788540)
XLA Ops:
  0.7 0.6 iota_divide_fusion
  1.3 0.6 fusion.78
  1.9 0.6 fusion.81
  2.5 1.4 add_select_fusion
  4.1 1.6 reshape.116
  5.6 2.0 broadcast_clamp_fusion
  7.6 6209.2 %gather_fusion = bf16[589824]{0:T(1024)(128)(2,1)} fusion(bf16[1536]{0:T(1024)(128)(2,1)S(1)} %pad_maximum_fusion, s32[589824]{0:T(1024)S(1)} %broadcast_clamp_fusion), kind=kCustom, calls=%fused_computation | custom fusion | bytes 4718592 | tf_op jit(solution)/shard_map/jit(_take)/gather | solution.py:22
  6216.9 2.6 reshape.115
  6219.5 1.2 fusion.10
  6220.7 1.0 copy-done.13
  6221.7 1.1 fusion.13
  6222.8 2.0 copy.40
  6224.8 10.5 all-to-all-start
  6235.4 23.3 all-to-all-done
  6259.0 0.3 copy.42
  6259.3 2.0 reshape.102
  6261.2 2.9 fusion.15
  6264.1 1.8 copy.84
  6266.0 5.0 all-to-all-start.1
  6270.9 0.9 constant_dynamic-slice_fusion
  6272.1 0.8 copy.38
  6272.9 0.9 tile.11
  6274.3 19.9 all-to-all-done.1
  6294.3 0.6 fusion.11
  6294.8 0.6 copy-done.1
  6295.4 0.7 copy.47
  6296.1 28.1 all_to_all.90
  6324.2 1.1 convolution_convert_fusion.2
  6325.3 2.0 copy.50
  6327.3 4.7 all-to-all-start.3
  6332.2 23.2 all-to-all-done.3
  6355.4 0.4 copy.117
  6355.8 0.8 copy.52
  6356.6 1.2 reshape.106
  6357.8 5.3 fusion.14
  6363.1 0.8 copy.54
  6363.9 28.2 all_to_all.91
  6392.3 0.3 copy.56
  6392.6 2.0 reshape.108
  6394.6 2.9 fusion.16
  6397.4 1.8 copy.90
  6399.3 5.2 all-to-all-start.5
  6404.8 23.2 all-to-all-done.5
  6428.0 2.5 convolution_bitcast_fusion
  6431.4 1.1 convert_element_type.150
  6432.5 7.3 all-to-all-start.8
  6439.7 2.0 fusion.12
  6441.8 1.8 copy.61
  6443.6 3.5 all-to-all-done.8
  6447.1 6.4 all-to-all-start.6
  6453.5 23.4 all-to-all-done.6
  6477.0 1.2 broadcast_in_dim.63
  6478.5 3.8 all-to-all-start.9
  6482.3 3.0 convolution_convert_fusion
  6485.3 2.0 copy.64
  6487.3 23.6 all-to-all-done.9
  6510.9 1.0 copy-done.3
  6511.8 6.9 all-to-all-start.7
  6518.7 2.6 reshape.113
  6521.3 20.7 all-to-all-done.7
  6542.1 0.4 copy.115
  6542.5 0.8 copy.66
  6543.3 1.2 reshape.112
  6544.5 4.1 fusion.1
  (57 shorter events, 3.2 us)
Async XLA Ops:
  0.6 6221.1 %copy-start = (bf16[1,6,768,128]{3,2,1,0:T(8,128)(2,1)S(1)}, bf16[1,6,768,128]{3,2,1,0:T(8,128)(2,1)}, u32[]{:S(2)}) copy-start(bf16[1,6,768,128]{3,2,1,0:T(8,128)(2,1)} %param.5) | copy-start | bytes 3538948
  6216.8 2.6 copy-start.6
  6216.8 2.6 copy-start.7
  6216.8 2.6 copy-start.8
  6216.8 2.6 copy-start.9
  6216.9 2.6 copy-start.10
  6216.9 2.6 copy-start.11
  6220.7 1.0 copy-start.13
  6224.8 10.5 copy-start.5
  6224.8 34.0 all-to-all-start
  6266.0 28.3 all-to-all-start.1
  6294.3 1.2 copy-start.1
  6296.1 28.1 copy-start.12
  6327.3 28.1 all-to-all-start.3
  6399.3 28.8 copy-start.2
  6399.3 28.8 all-to-all-start.5
  6432.5 14.6 all-to-all-start.8
  6447.1 29.9 all-to-all-start.6
  6477.0 1.5 copy-start.4
  6478.5 32.4 all-to-all-start.9
  6510.9 1.0 copy-start.3
  6511.8 30.2 all-to-all-start.7
